TPU v7x, 32 devices: a whole 2x2x4 slice. The times are simulated.
32 devices in a mesh: req: 8 (over z, y), tp: 4 (over x, core).
Axes of the slice: x: 2, y: 2, z: 4, core: 2. Of those that a mesh axis runs over, the one named last changes fastest.
Arguments:
- hidden: bfloat16 [4096, 2048], P('req', 'tp'), may hold values from -6 to 6
- queries: bfloat16 [4096, 2048], P('req', 'tp'), may hold values from -4 to 4
- new_keys: bfloat16 [4096, 512], P('req'), may hold values from -4 to 4
- new_values: bfloat16 [4096, 512], P('req'), may hold values from -6 to 6
- cache_keys: bfloat16 [384, 64, 512], P('req'), may hold values from -6 to 6
- cache_values: bfloat16 [384, 64, 512], P('req'), may hold values from -6 to 6
- out_weight: bfloat16 [2048, 2048], P('tp'), may hold values from -0.125 to 0.125
- attn_gain: bfloat16 [2048], P('tp'), may hold values from 0.099609375 to 1.8984375
- ple_input: bfloat16 [4096, 256], P('req'), may hold values from -6 to 6
- ple_gate_weight: bfloat16 [2048, 256], P('tp'), may hold values from -0.125 to 0.125
- ple_proj_weight: bfloat16 [256, 2048], P(None, 'tp'), may hold values from -0.375 to 0.375
- ple_gain: bfloat16 [2048], P('tp'), may hold values from 0.099609375 to 1.8984375
- page_holder: int32 [384, 1], P('req'), may hold values from 0 to 7; in each aligned block of 48 rows (0 to 47, 48 to 95, ...) at most 6 rows name the same one
- page_slot: int32 [384, 1], P('req'), may hold values from 0 to 47
- page_counts: int32 [8, 8], P('req'), may hold values from 1 to 12, 48 in all within a row
- last_fill: int32 [8, 8], P('req'), may hold values from 1 to 64
- row_counts: int32 [8, 8], P('req'), may hold values from 1 to 256, 512 in all within a row
Outputs:
- layer_out: bfloat16 [4096, 2048], P('req', 'tp')
Inputs may be any that keep to these rules, and one draw needn't show every extreme that they name: `page_holder`: within the 48 page references of one device's requests (aligned blocks), no req index is named more than 6 times; in some block one is named exactly 6 times. `page_counts`: the 8 counts of one device sum to 48; some count equals 12. `row_counts`: the 8 counts of one device sum to 512; some count equals 256.
All inputs are finite; a program needn't handle non-finite values.
Results may differ from a plain program's by a relative error of at most 0.0061.
Values may be sent and summed in bfloat16 or wider, within the bound.
No kernel may reach another device: no remote copies, remote signals or barrier semaphores. Data moves between devices by JAX's collectives and lax.ppermute only.
A program may use at most 128 MiB of HBM per device.

v0:
```python
import math
import jax
import jax.numpy as jnp
from jax import lax
from jax.sharding import PartitionSpec as P

D = 2048
HD = 256


def slot_lookup(positions, counts):
    starts = jnp.cumsum(counts) - counts
    owning = jnp.sum((positions[:, None] >= starts[None, :]).astype(jnp.int32), axis=1) - 1
    return (owning, starts)


def table_pick(table, owning):
    onehot = owning[:, None] == jnp.arange(table.shape[0], dtype=jnp.int32)[None, :]
    return jnp.sum(jnp.where(onehot, table[None, :], 0), axis=1)


def attend_masks(counts_of_pages, fill_row, counts_of_rows, page_len, page_total, row_total):
    key_index = jnp.arange(page_total * page_len, dtype=jnp.int32)
    page_ref = key_index // page_len
    within = key_index % page_len
    page_owner, page_starts = slot_lookup(page_ref, counts_of_pages)
    context_len = (counts_of_pages - 1) * page_len + fill_row
    position = (page_ref - table_pick(page_starts, page_owner)) * page_len + within
    valid = position < table_pick(context_len, page_owner)
    row_index = jnp.arange(row_total, dtype=jnp.int32)
    row_owner = slot_lookup(row_index, counts_of_rows)[0]
    context_mask = (row_owner[:, None] == page_owner[None, :]) & valid[None, :]
    causal = (row_owner[:, None] == row_owner[None, :]) & (row_index[None, :] <= row_index[:, None])
    return jnp.concatenate([context_mask, causal], axis=1)


def shards(
    hidden,
    queries,
    new_keys,
    new_values,
    cache_keys,
    cache_values,
    out_weight,
    attn_gain,
    ple_input,
    ple_gate_weight,
    ple_proj_weight,
    ple_gain,
    page_holder,
    page_slot,
    page_counts,
    last_fill,
    row_counts,
):
    row_total = hidden.shape[0]
    page_total = cache_keys.shape[0]
    page_len = cache_keys.shape[1]
    req_count = lax.axis_size("req")
    tp_index = lax.axis_index("tp")
    local_heads = queries.shape[1] // HD
    kv_head = tp_index // 2
    capacity = max(2, page_total // req_count)
    holders = page_holder[:, 0]
    places = page_slot[:, 0]
    ref_index = jnp.arange(page_total, dtype=jnp.int32)
    earlier = (holders[:, None] == holders[None, :]) & (ref_index[:, None] > ref_index[None, :])
    ranking = jnp.sum(earlier.astype(jnp.int32), axis=1)
    matched = (holders[:, None, None] == jnp.arange(req_count, dtype=jnp.int32)[None, :, None]) & (
        ranking[:, None, None] == jnp.arange(capacity, dtype=jnp.int32)[None, None, :]
    )
    request_table = jnp.sum(jnp.where(matched, places[:, None, None] + 1, 0), axis=0) - 1
    asked = lax.all_to_all(request_table, "req", split_axis=0, concat_axis=0, tiled=True)
    wanted = jnp.maximum(asked, 0)
    head_keys = lax.dynamic_slice_in_dim(cache_keys, kv_head * HD, HD, 2)
    head_values = lax.dynamic_slice_in_dim(cache_values, kv_head * HD, HD, 2)
    stacked = jnp.concatenate([head_keys, head_values], axis=2)
    arrival_index = holders * capacity + ranking
    outgoing = stacked[wanted]
    arrived = lax.all_to_all(outgoing, "req", split_axis=0, concat_axis=0, tiled=True)
    context = arrived.reshape(req_count * capacity, page_len, 2 * HD)[arrival_index]
    context_keys = context[:, :, :HD].reshape(page_total * page_len, HD)
    context_values = context[:, :, HD:].reshape(page_total * page_len, HD)
    fresh_keys = lax.dynamic_slice_in_dim(new_keys, kv_head * HD, HD, 1)
    fresh_values = lax.dynamic_slice_in_dim(new_values, kv_head * HD, HD, 1)
    all_keys = jnp.concatenate([context_keys, fresh_keys], axis=0)
    all_values = jnp.concatenate([context_values, fresh_values], axis=0)
    masking = attend_masks(
        page_counts[0], last_fill[0], row_counts[0], page_len, page_total, row_total
    )
    query_rows = queries.reshape(row_total, local_heads, HD)
    scores = jnp.einsum("rhd,kd->hrk", query_rows, all_keys, preferred_element_type=jnp.float32) * (
        1.0 / math.sqrt(HD)
    )
    scores = jnp.where(masking[None], scores, -1e30)
    highest = jnp.max(scores, axis=-1, keepdims=True)
    expo = jnp.exp(scores - highest)
    weights = (expo / jnp.sum(expo, axis=-1, keepdims=True)).astype(jnp.bfloat16)
    attention = jnp.einsum("hrk,kd->rhd", weights, all_values, preferred_element_type=jnp.float32)
    attention = attention.astype(jnp.bfloat16).reshape(row_total, local_heads * HD)
    tp_size = lax.axis_size("tp")
    full_weight = lax.all_gather(out_weight, "tp", axis=0, tiled=True)
    full_gate_weight = lax.all_gather(ple_gate_weight, "tp", axis=0, tiled=True)
    full_proj_weight = lax.all_gather(ple_proj_weight, "tp", axis=1, tiled=True)
    full_attn_gain = lax.all_gather(attn_gain, "tp", axis=0, tiled=True)
    full_ple_gain = lax.all_gather(ple_gain, "tp", axis=0, tiled=True)
    row_hidden = lax.all_to_all(hidden, "tp", split_axis=0, concat_axis=1, tiled=True)
    row_attention = lax.all_to_all(attention, "tp", split_axis=0, concat_axis=1, tiled=True)
    part_rows = row_attention.shape[0]
    row_ple = lax.dynamic_slice_in_dim(ple_input, tp_index * part_rows, part_rows, 0)
    projected = jnp.dot(row_attention, full_weight, preferred_element_type=jnp.float32)
    squares = jnp.sum(projected * projected, axis=1)
    normed = (
        projected
        * lax.rsqrt(squares / D + 1e-06)[:, None]
        * full_attn_gain.astype(jnp.float32)[None, :]
    )
    mixed_state = (row_hidden.astype(jnp.float32) + normed).astype(jnp.bfloat16)
    gate = jnp.dot(mixed_state, full_gate_weight, preferred_element_type=jnp.float32)
    activated = (jax.nn.gelu(gate, approximate=True) * row_ple.astype(jnp.float32)).astype(
        jnp.bfloat16
    )
    lifted = jnp.dot(activated, full_proj_weight, preferred_element_type=jnp.float32)
    lift_squares = jnp.sum(lifted * lifted, axis=1)
    lift_normed = (
        lifted
        * lax.rsqrt(lift_squares / D + 1e-06)[:, None]
        * full_ple_gain.astype(jnp.float32)[None, :]
    )
    row_out = (mixed_state.astype(jnp.float32) + lift_normed).astype(jnp.bfloat16)
    return lax.all_to_all(row_out, "tp", split_axis=1, concat_axis=0, tiled=True)


def solution(mesh):
    return jax.shard_map(
        shards,
        mesh=mesh,
        in_specs=(
            P("req", "tp"),
            P("req", "tp"),
            P("req", None),
            P("req", None),
            P("req", None, None),
            P("req", None, None),
            P("tp", None),
            P("tp"),
            P("req", None),
            P("tp", None),
            P(None, "tp"),
            P("tp"),
            P("req", None),
            P("req", None),
            P("req", None),
            P("req", None),
            P("req", None),
        ),
        out_specs=P("req", "tp"),
        check_vma=False,
    )
```

profile of v0, /device:TPU:0, one launch (start us, length us, event | category | flops | bytes accessed | tf_op | source)
XLA Modules:
  0.0 189.8 jit_solution(16006355638064620231)
XLA Ops:
  7.3 0.9 convert_reduce_fusion.1
  10.4 7.3 %all-to-all-start.1 = ((s32[8,1,6]{2,1,0:T(1,128)}), s32[8,1,6]{2,1,0:T(1,128)S(1)}, u32[]{:S(2)}, u32[]{:S(2)}) async-start(s32[8,1,6]{2,1,0:T(1,128)} %copy.41), calls=%async_computation.1 | async-start | bytes 8192 | tf_op jit(solution)/shard_map/all_to_all | solution.py:73
  17.7 2.7 %constant_dynamic-slice_fusion.2 = (bf16[48,64,256]{2,1,0:T(8,128)(2,1)S(1)}, bf16[48,64,256]{2,1,0:T(8,128)(2,1)S(1)}) fusion(bf16[48,64,512]{2,1,0:T(8,128)(2,1)} %param.22, s32[]{:T(128)S(6)} %select_n.60, bf16[48,64,512]{2,1,0:T(8,128)(2,1)} %param.21), kind=kLoop, calls=%fused_computation.83 | loop fusion | bytes 6291460 | tf_op jit(solution)/shard_map/dynamic_slice | solution.py:76
  20.6 3.4 %all-to-all-done.1 = s32[8,1,6]{2,1,0:T(1,128)S(1)} async-done(((s32[8,1,6]{2,1,0:T(1,128)}), s32[8,1,6]{2,1,0:T(1,128)S(1)}, u32[]{:S(2)}, u32[]{:S(2)}) %all-to-all-start.1) | async-done | bytes 224 | tf_op jit(solution)/shard_map/all_to_all | solution.py:73
  24.2 2.5 %gather_fusion = bf16[48,64,512]{2,1,0:T(8,128)(2,1)} fusion(bf16[48,64,512]{2,1,0:T(8,128)(2,1)S(1)} %pad_maximum_fusion, s32[1024]{0:T(1024)S(1)} %pad_clamp_fusion.1), kind=kCustom, calls=%fused_computation | custom fusion | bytes 6291648 | tf_op jit(solution)/shard_map/gather | solution.py:79
  26.7 3.8 %all-to-all-start.2 = ((bf16[8,6,64,512]{3,2,1,0:T(8,128)(2,1)}), bf16[8,6,64,512]{3,2,1,0:T(8,128)(2,1)S(1)}, u32[]{:S(2)}, u32[]{:S(2)}) async-start(bf16[8,6,64,512]{3,2,1,0:T(8,128)(2,1)} %bitcast.73), calls=%async_computation.2 | async-start | bytes 6291456 | tf_op jit(solution)/shard_map/all_to_all | solution.py:80
  31.6 1.8 constant_dynamic-slice_fusion
  34.8 2.4 %compare_and_fusion = pred[512,3072]{0,1:T(8,128)(4,1)S(1)} fusion(s32[512]{0:T(512)S(1)} %broadcast_add_fusion.1, s32[3072]{0:T(1024)S(1)} %broadcast_add_fusion, pred[3072]{0:T(1024)(128)(4,1)S(1)} %fusion.40), kind=kLoop, calls=%fused_computation.12 | loop fusion | flops 3145728 | bytes 1590272 | tf_op jit(solution)/shard_map/and | solution.py:32
  37.2 1.7 pad_add_fusion
  38.9 61.1 %all-to-all-done.2 = bf16[8,6,64,512]{3,2,1,0:T(8,128)(2,1)S(1)} async-done(((bf16[8,6,64,512]{3,2,1,0:T(8,128)(2,1)}), bf16[8,6,64,512]{3,2,1,0:T(8,128)(2,1)S(1)}, u32[]{:S(2)}, u32[]{:S(2)}) %all-to-all-start.2) | async-done | bytes 3145760 | tf_op jit(solution)/shard_map/all_to_all | solution.py:80
  100.0 4.1 %all-to-all-start = ((bf16[4,128,512]{2,1,0:T(8,128)(2,1)}), bf16[4,128,512]{2,1,0:T(8,128)(2,1)}, u32[]{:S(2)}, u32[]{:S(2)}) async-start(bf16[4,128,512]{2,1,0:T(8,128)(2,1)} %bitcast.82), calls=%async_computation | async-start | bytes 1048576 | tf_op jit(solution)/shard_map/all_to_all | solution.py:107
  104.1 2.5 %gather_fusion.1 = bf16[48,64,512]{2,1,0:T(8,128)(2,1)} fusion(bf16[48,64,512]{2,1,0:T(8,128)(2,1)S(1)} %bitcast.72, s32[1024]{0:T(1024)S(1)} %pad_clamp_fusion), kind=kCustom, calls=%fused_computation.1 | custom fusion | bytes 6291648 | tf_op jit(solution)/shard_map/gather | solution.py:81
  106.6 2.1 %fusion.52 = (bf16[48,64,256]{2,1,0:T(8,128)(2,1)S(1)}, bf16[48,64,256]{2,1,0:T(8,128)(2,1)S(1)}) fusion(bf16[48,64,512]{2,1,0:T(8,128)(2,1)} %gather_fusion.1), kind=kLoop, calls=%fused_computation.102 | loop fusion | bytes 6291456 | tf_op jit(solution)/shard_map/slice | solution.py:83
  108.7 1.8 copy.43
  110.5 8.6 %fusion.8 = f32[3584,512,2]{1,0,2:T(8,128)} fusion(bf16[512,256]{1,0:T(8,128)(2,1)} %get-tuple-element.17, bf16[3072,256]{1,0:T(8,128)(2,1)S(1)} %bitcast.74, bf16[64,2,8,256]{3,2,1,0:T(8,128)(2,1)} %bitcast.81), kind=kOutput, calls=%fused_computation.18 | convolution fusion | flops 1882718208 | bytes 17039360 | tf_op jit(solution)/shard_map/rhd,kd->hrk/dot_general | solution.py:92
  119.1 16.0 %fusion.53 = (f32[2,512]{1,0:T(2,128)S(1)}, f32[2,512,3584]{1,2,0:T(8,128)}) fusion(f32[3584,512,2]{1,0,2:T(8,128)} %fusion.8, pred[512,3584]{0,1:T(8,128)(4,1)S(1)} %copy-done), kind=kOutput, calls=%fused_computation.103 | output fusion | flops 22023680 | bytes 31199232 | tf_op jit(solution)/shard_map/sub | solution.py:97
  135.0 7.3 %fusion.12 = bf16[512,2,256]{0,2,1:T(8,128)(2,1)S(1)} fusion(f32[2,512,3584]{1,2,0:T(8,128)} %get-tuple-element.12, f32[2,512]{1,0:T(2,128)S(1)} %get-tuple-element.11, bf16[512,256]{0,1:T(8,128)(2,1)} %copy.51, bf16[3072,256]{0,1:T(8,128)(2,1)S(1)} %copy-done.1), kind=kOutput, calls=%fused_computation.22 | convolution fusion | flops 1890320384 | bytes 17043456 | tf_op jit(solution)/shard_map/hrk,kd->rhd/dot_general | solution.py:99
  143.4 3.7 %all-to-all-start.3 = ((bf16[4,128,512]{1,2,0:T(8,128)(2,1)}), bf16[4,128,512]{1,2,0:T(8,128)(2,1)S(1)}, u32[]{:S(2)}, u32[]{:S(2)}) async-start(bf16[4,128,512]{1,2,0:T(8,128)(2,1)} %copy.46), calls=%async_computation.3 | async-start | bytes 1048576 | tf_op jit(solution)/shard_map/all_to_all | solution.py:108
  147.8 9.0 %all-gather = bf16[4,1,512]{2,1,0:T(2,128)(2,1)S(1)} all-gather(bf16[1,1,512]{2,1,0:T(2,128)(2,1)S(1)} %reshape.210), channel_id=1, replica_groups=mesh['req'=8,'tp'=4] {'tp'}, dimensions={0}, use_global_device_ids=true | all-gather | bytes 5120 | tf_op jit(solution)/shard_map/all_gather | solution.py:105
  156.8 5.2 %all-gather.1 = bf16[4,1,512]{2,1,0:T(2,128)(2,1)S(1)} all-gather(bf16[1,1,512]{2,1,0:T(2,128)(2,1)S(1)} %reshape.212), channel_id=1, replica_groups=mesh['req'=8,'tp'=4] {'tp'}, dimensions={0}, use_global_device_ids=true | all-gather | bytes 5120 | tf_op jit(solution)/shard_map/all_gather | solution.py:106
  162.0 1.2 convert_bitcast_fusion
  163.4 4.8 %multiply_reduce_fusion.1 = (f32[128]{0:T(128)S(1)}, f32[128,2048]{1,0:T(8,128)S(1)}) fusion(bf16[128,2048]{0,1:T(8,128)(2,1)S(1)} %bitcast.77, bf16[2048,2048]{1,0:T(8,128)(2,1)} %all-gather.6.cloned.1.call-done), kind=kOutput, calls=%fused_computation.27 | convolution fusion | flops 1074265984 | bytes 9961984 | tf_op jit(solution)/shard_map/dot_general | solution.py:111
  168.4 2.5 %multiply_reduce_fusion = (f32[128]{0:T(128)S(1)}, f32[128,2048]{1,0:T(8,128)S(1)}) fusion(bf16[256,2048]{1,0:T(8,128)(2,1)} %all-gather.10.cloned.1.call-done, bf16[512,256]{1,0:T(8,128)(2,1)} %param.25, s32[]{:T(128)S(6)} %select_n.68, bf16[128,2048]{1,0:T(8,128)(2,1)S(1)} %add_convert_fusion.1, bf16[2048,256]{1,0:T(8,128)(2,1)} %all-gather.8.cloned.1.call-done), kind=kOutput, calls=%fused_computation.25 | convolution fusion | flops 269320064 | bytes 3736068 | tf_op jit(solution)/shard_map/dot_general | solution.py:123
  171.2 11.2 %all_to_all.62 = bf16[128,4,512]{2,0,1:T(8,128)(2,1)S(1)} all-to-all(bf16[128,4,512]{2,0,1:T(8,128)(2,1)S(1)} %bitcast.79), channel_id=1, replica_groups=mesh['req'=8,'tp'=4] {'tp'}, dimensions={1} | all-to-all | bytes 1048576 | tf_op jit(solution)/shard_map/all_to_all | solution.py:131
  (65 shorter events, 9.0 us)
Async XLA Ops:
  6.5 156.8 %all-gather.6.cloned.1.call-start = ((), (), s32[]{:S(2)}) async-start(), calls=%async_computation.5 | async-start | bytes 10485760 | tf_op jit(solution)/shard_map/all_gather | solution.py:102
  10.4 13.7 %all-to-all-start.1 = ((s32[8,1,6]{2,1,0:T(1,128)}), s32[8,1,6]{2,1,0:T(1,128)S(1)}, u32[]{:S(2)}, u32[]{:S(2)}) async-start(s32[8,1,6]{2,1,0:T(1,128)} %copy.41), calls=%async_computation.1 | async-start | bytes 8192 | tf_op jit(solution)/shard_map/all_to_all | solution.py:73
  26.7 4.6 %copy-start.5 = (s32[1,8]{1,0:T(1,128)S(1)}, s32[1,8]{1,0:T(1,128)}, u32[]{:S(2)}) copy-start(s32[1,8]{1,0:T(1,128)} %param.31) | copy-start | bytes 100
  26.7 4.8 %copy-start.7 = (s32[1,8]{1,0:T(1,128)S(1)}, s32[1,8]{1,0:T(1,128)}, u32[]{:S(2)}) copy-start(s32[1,8]{1,0:T(1,128)} %param.33) | copy-start | bytes 100
  26.7 7.5 %copy-start.6 = (s32[48,1]{0,1:T(1,128)S(1)}, s32[48,1]{0,1:T(1,128)}, u32[]{:S(2)}) copy-start(s32[48,1]{0,1:T(1,128)} %param.29) | copy-start | bytes 580
  26.7 7.7 %copy-start.4 = (s32[1,8]{1,0:T(1,128)S(1)}, s32[1,8]{1,0:T(1,128)}, u32[]{:S(2)}) copy-start(s32[1,8]{1,0:T(1,128)} %param.32) | copy-start | bytes 100
  26.7 73.3 %all-to-all-start.2 = ((bf16[8,6,64,512]{3,2,1,0:T(8,128)(2,1)}), bf16[8,6,64,512]{3,2,1,0:T(8,128)(2,1)S(1)}, u32[]{:S(2)}, u32[]{:S(2)}) async-start(bf16[8,6,64,512]{3,2,1,0:T(8,128)(2,1)} %bitcast.73), calls=%async_computation.2 | async-start | bytes 6291456 | tf_op jit(solution)/shard_map/all_to_all | solution.py:80
  30.5 137.9 %all-gather.10.cloned.1.call-start = ((), (), s32[]{:S(2)}) async-start(), calls=%async_computation.7 | async-start | bytes 1310720 | tf_op jit(solution)/shard_map/all_gather | solution.py:104
  100.0 43.4 %all-to-all-start = ((bf16[4,128,512]{2,1,0:T(8,128)(2,1)}), bf16[4,128,512]{2,1,0:T(8,128)(2,1)}, u32[]{:S(2)}, u32[]{:S(2)}) async-start(bf16[4,128,512]{2,1,0:T(8,128)(2,1)} %bitcast.82), calls=%async_computation | async-start | bytes 1048576 | tf_op jit(solution)/shard_map/all_to_all | solution.py:107
  110.5 8.6 %copy-start = (pred[512,3584]{0,1:T(8,128)(4,1)S(1)}, pred[512,3584]{0,1:T(8,128)(4,1)}, u32[]{:S(2)}) copy-start(pred[512,3584]{0,1:T(8,128)(4,1)} %pad_add_fusion) | copy-start | bytes 5505028
  119.1 16.0 %copy-start.1 = (bf16[3072,256]{0,1:T(8,128)(2,1)S(1)}, bf16[3072,256]{0,1:T(8,128)(2,1)}, u32[]{:S(2)}) copy-start(bf16[3072,256]{0,1:T(8,128)(2,1)} %copy.43) | copy-start | bytes 4718596
  142.4 5.4 %copy-start.2 = (bf16[512]{0:T(512)(128)(2,1)S(1)}, bf16[512]{0:T(512)(128)(2,1)}, u32[]{:S(2)}) copy-start(bf16[512]{0:T(512)(128)(2,1)} %param.24) | copy-start | bytes 3076
  142.4 14.4 %copy-start.3 = (bf16[512]{0:T(512)(128)(2,1)S(1)}, bf16[512]{0:T(512)(128)(2,1)}, u32[]{:S(2)}) copy-start(bf16[512]{0:T(512)(128)(2,1)} %param.28) | copy-start | bytes 3076
  143.4 19.9 %all-to-all-start.3 = ((bf16[4,128,512]{1,2,0:T(8,128)(2,1)}), bf16[4,128,512]{1,2,0:T(8,128)(2,1)S(1)}, u32[]{:S(2)}, u32[]{:S(2)}) async-start(bf16[4,128,512]{1,2,0:T(8,128)(2,1)} %copy.46), calls=%async_computation.3 | async-start | bytes 1048576 | tf_op jit(solution)/shard_map/all_to_all | solution.py:108
  147.1 21.4 %all-gather.8.cloned.1.call-start = ((), (), s32[]{:S(2)}) async-start(), calls=%async_computation.6 | async-start | bytes 1310720 | tf_op jit(solution)/shard_map/all_gather | solution.py:103
Sparse Core Ops, SparseCore 0:
  8.9 60.9 all-gather.5
  71.5 16.7 all-gather.9
  149.5 16.2 all-gather.7
where the time goes:
time: 190 us
  waiting for transfers between devices  66.7 us (35%)
  blocking collectives  25.4 us (13%)
  other arithmetic  25.3 us (13%)
  matrix products  23.1 us (12%)
  starting transfers between devices  19 us (10%)
  local copies, waits for them, and re-layouts  16.9 us (9%)
  between operations  13.4 us (7%)
    all_to_all x1, waiting for transfers between devices, shards(): lax.all_to_all(outgoing, 'req', split_axis=0, concat_axis=0, tiled=True)  61.1 us
    sub x1, other arithmetic, shards(): expo = jnp.exp(scores - highest)  16 us
    all_to_all x1, blocking collectives, shards(): lax.all_to_all(row_out, 'tp', split_axis=1, concat_axis=0, tiled=True)  11.2 us
    all_gather x1, blocking collectives, shards(): full_attn_gain = lax.all_gather(attn_gain, 'tp', axis=0, tiled=True)  8.99 us
    dot_general x1, matrix products, shards(): jnp.einsum('rhd,kd->hrk', query_rows, all_keys, preferred_element_type=jn...  8.55 us
    dot_general x1, matrix products, shards(): jnp.einsum('hrk,kd->rhd', weights, all_values, preferred_element_type=jnp...  7.33 us
    all_to_all x1, starting transfers between devices, shards(): lax.all_to_all(request_table, 'req', split_axis=0, concat_axis=0, tiled=T...  7.28 us
    all_gather x1, blocking collectives, shards(): full_ple_gain = lax.all_gather(ple_gain, 'tp', axis=0, tiled=True)  5.18 us
  transfers between devices with their start and end apart: 7, of which 2 were waited for; matrix products, arithmetic and copies ran while one was open for 32% of the time, Pallas kernels for 0%

commit v1 on v0

--- a/solution.py
+++ b/solution.py
@@ -104,7 +104,19 @@
     full_proj_weight = lax.all_gather(ple_proj_weight, "tp", axis=1, tiled=True)
     full_attn_gain = lax.all_gather(attn_gain, "tp", axis=0, tiled=True)
     full_ple_gain = lax.all_gather(ple_gain, "tp", axis=0, tiled=True)
-    row_hidden = lax.all_to_all(hidden, "tp", split_axis=0, concat_axis=1, tiled=True)
+    ways, here = (lax.axis_size("tp"), lax.axis_index("tp"))
+    width = hidden.shape[0] // ways
+    shape = list(hidden.shape)
+    shape[0] = width
+    height = shape[1]
+    shape[1] = height * ways
+    full = jnp.zeros(shape, hidden.dtype)
+    for mask in range(ways):
+        part = lax.dynamic_slice_in_dim(hidden, (here ^ mask) * width, width, axis=0)
+        if mask:
+            part = lax.ppermute(part, "tp", [(d, d ^ mask) for d in range(ways)])
+        full = lax.dynamic_update_slice_in_dim(full, part, (here ^ mask) * height, axis=1)
+    row_hidden = full
     row_attention = lax.all_to_all(attention, "tp", split_axis=0, concat_axis=1, tiled=True)
     part_rows = row_attention.shape[0]
     row_ple = lax.dynamic_slice_in_dim(ple_input, tp_index * part_rows, part_rows, 0)

time: 190 us -> 197 us (1.037)
  blocking collectives: 25.4 us -> 33.1 us
  waiting for transfers between devices: 66.7 us -> 61.4 us
  local copies, waits for them, and re-layouts: 16.9 us -> 21.6 us
  starting transfers between devices: 19 us -> 16.6 us
    all_gather x1, blocking collectives: 8.99 us -> 16.5 us  [shards(): full_attn_gain = lax.all_gather(attn_gain, 'tp', axis=0, tiled=True)]
    all_to_all x1 -> x0, starting transfers between devices: 4.14 us -> none  [shards(): lax.all_to_all(hidden, 'tp', split_axis=0, concat_axis=1, tiled=True)]
    all_to_all x1, waiting for transfers between devices: 61.1 us -> 57.2 us  [shards(): lax.all_to_all(outgoing, 'req', split_axis=0, concat_axis=0, tiled=True)]
    dynamic_update_slice x0 -> x3, local copies, waits for them, and re-layouts: none -> 2.05 us  [shards(): lax.dynamic_update_slice_in_dim(full, part, (here ^ mask) * height, axis=1)]
  transfers between devices with their start and end apart: 7 -> 9, of which waited for: 2 -> 2; matrix products, arithmetic and copies ran while one was open for 32% -> 35% of each run, Pallas kernels for 0% -> 0%
where the time goes in v1:
time: 197 us; the launch traced here: 196 us
  waiting for transfers between devices  61.4 us (31%)
  blocking collectives  33.1 us (17%)
  other arithmetic  27 us (14%)
  matrix products  23.1 us (12%)
  local copies, waits for them, and re-layouts  21.6 us (11%)
  starting transfers between devices  16.6 us (8%)
  between operations  13.5 us (7%)
    all_to_all x1, waiting for transfers between devices, shards(): lax.all_to_all(outgoing, 'req', split_axis=0, concat_axis=0, tiled=True)  57.2 us
    all_gather x1, blocking collectives, shards(): full_attn_gain = lax.all_gather(attn_gain, 'tp', axis=0, tiled=True)  16.5 us
    sub x1, other arithmetic, shards(): expo = jnp.exp(scores - highest)  16 us
    all_to_all x1, blocking collectives, shards(): lax.all_to_all(row_out, 'tp', split_axis=1, concat_axis=0, tiled=True)  11.2 us
    dot_general x1, matrix products, shards(): jnp.einsum('rhd,kd->hrk', query_rows, all_keys, preferred_element_type=jn...  8.55 us
    dot_general x1, matrix products, shards(): jnp.einsum('hrk,kd->rhd', weights, all_values, preferred_element_type=jnp...  7.34 us
    all_to_all x1, starting transfers between devices, shards(): lax.all_to_all(request_table, 'req', split_axis=0, concat_axis=0, tiled=T...  7.28 us
    all_gather x1, blocking collectives, shards(): full_ple_gain = lax.all_gather(ple_gain, 'tp', axis=0, tiled=True)  5.35 us
  transfers between devices with their start and end apart: 9, of which 2 were waited for; matrix products, arithmetic and copies ran while one was open for 35% of the time, Pallas kernels for 0%

profile of v1, /device:TPU:0, one launch (start us, length us, event | category | flops | bytes accessed | tf_op | source)
XLA Modules:
  0.0 196.3 jit_solution(14978938276825330772)
XLA Ops:
  10.4 7.3 %all-to-all-start = ((s32[8,1,6]{2,1,0:T(1,128)}), s32[8,1,6]{2,1,0:T(1,128)S(1)}, u32[]{:S(2)}, u32[]{:S(2)}) async-start(s32[8,1,6]{2,1,0:T(1,128)} %copy.37), calls=%async_computation | async-start | bytes 8192 | tf_op jit(solution)/shard_map/all_to_all | solution.py:73
  17.7 2.7 %constant_dynamic-slice_fusion.2 = (bf16[48,64,256]{2,1,0:T(8,128)(2,1)S(1)}, bf16[48,64,256]{2,1,0:T(8,128)(2,1)S(1)}) fusion(bf16[48,64,512]{2,1,0:T(8,128)(2,1)} %param.22, s32[]{:T(128)S(6)} %select_n.90, bf16[48,64,512]{2,1,0:T(8,128)(2,1)} %param.21), kind=kLoop, calls=%fused_computation.82 | loop fusion | bytes 6291460 | tf_op jit(solution)/shard_map/dynamic_slice | solution.py:76
  20.6 3.4 %all-to-all-done = s32[8,1,6]{2,1,0:T(1,128)S(1)} async-done(((s32[8,1,6]{2,1,0:T(1,128)}), s32[8,1,6]{2,1,0:T(1,128)S(1)}, u32[]{:S(2)}, u32[]{:S(2)}) %all-to-all-start) | async-done | bytes 224 | tf_op jit(solution)/shard_map/all_to_all | solution.py:73
  24.2 2.5 %gather_fusion = bf16[48,64,512]{2,1,0:T(8,128)(2,1)} fusion(bf16[48,64,512]{2,1,0:T(8,128)(2,1)S(1)} %pad_maximum_fusion, s32[1024]{0:T(1024)S(1)} %pad_clamp_fusion.1), kind=kCustom, calls=%fused_computation | custom fusion | bytes 6291648 | tf_op jit(solution)/shard_map/gather | solution.py:79
  26.7 3.8 %all-to-all-start.1 = ((bf16[8,6,64,512]{3,2,1,0:T(8,128)(2,1)}), bf16[8,6,64,512]{3,2,1,0:T(8,128)(2,1)S(1)}, u32[]{:S(2)}, u32[]{:S(2)}) async-start(bf16[8,6,64,512]{3,2,1,0:T(8,128)(2,1)} %bitcast.68), calls=%async_computation.1 | async-start | bytes 6291456 | tf_op jit(solution)/shard_map/all_to_all | solution.py:80
  31.4 1.9 constant_dynamic-slice_fusion.4
  34.2 1.8 constant_dynamic-slice_fusion
  38.7 2.4 %compare_and_fusion = pred[512,3072]{0,1:T(8,128)(4,1)S(1)} fusion(s32[512]{0:T(512)S(1)} %broadcast_add_fusion.1, s32[3072]{0:T(1024)S(1)} %broadcast_add_fusion, pred[3072]{0:T(1024)(128)(4,1)S(1)} %fusion.40), kind=kLoop, calls=%fused_computation.12 | loop fusion | flops 3145728 | bytes 1590272 | tf_op jit(solution)/shard_map/and | solution.py:32
  41.1 1.7 pad_add_fusion
  42.7 57.2 %all-to-all-done.1 = bf16[8,6,64,512]{3,2,1,0:T(8,128)(2,1)S(1)} async-done(((bf16[8,6,64,512]{3,2,1,0:T(8,128)(2,1)}), bf16[8,6,64,512]{3,2,1,0:T(8,128)(2,1)S(1)}, u32[]{:S(2)}, u32[]{:S(2)}) %all-to-all-start.1) | async-done | bytes 3145760 | tf_op jit(solution)/shard_map/all_to_all | solution.py:80
  99.9 2.5 %gather_fusion.1 = bf16[48,64,512]{2,1,0:T(8,128)(2,1)} fusion(bf16[48,64,512]{2,1,0:T(8,128)(2,1)S(1)} %bitcast.67, s32[1024]{0:T(1024)S(1)} %pad_clamp_fusion), kind=kCustom, calls=%fused_computation.1 | custom fusion | bytes 6291648 | tf_op jit(solution)/shard_map/gather | solution.py:81
  102.5 2.1 %fusion.52 = (bf16[48,64,256]{2,1,0:T(8,128)(2,1)S(1)}, bf16[48,64,256]{2,1,0:T(8,128)(2,1)S(1)}) fusion(bf16[48,64,512]{2,1,0:T(8,128)(2,1)} %gather_fusion.1), kind=kLoop, calls=%fused_computation.108 | loop fusion | bytes 6291456 | tf_op jit(solution)/shard_map/slice | solution.py:83
  104.6 1.8 copy.39
  106.3 8.6 %fusion.8 = f32[3584,512,2]{1,0,2:T(8,128)} fusion(bf16[512,256]{1,0:T(8,128)(2,1)} %get-tuple-element.22, bf16[3072,256]{1,0:T(8,128)(2,1)S(1)} %bitcast.69, bf16[64,2,8,256]{3,2,1,0:T(8,128)(2,1)} %bitcast.75), kind=kOutput, calls=%fused_computation.18 | convolution fusion | flops 1882718208 | bytes 17039360 | tf_op jit(solution)/shard_map/rhd,kd->hrk/dot_general | solution.py:92
  114.9 16.0 %fusion.53 = (f32[2,512]{1,0:T(2,128)S(1)}, f32[2,512,3584]{1,2,0:T(8,128)}) fusion(f32[3584,512,2]{1,0,2:T(8,128)} %fusion.8, pred[512,3584]{0,1:T(8,128)(4,1)S(1)} %copy-done), kind=kOutput, calls=%fused_computation.109 | output fusion | flops 22023680 | bytes 31199232 | tf_op jit(solution)/shard_map/sub | solution.py:97
  130.9 7.3 %fusion.12 = bf16[512,2,256]{0,2,1:T(8,128)(2,1)S(1)} fusion(f32[2,512,3584]{1,2,0:T(8,128)} %get-tuple-element.16, f32[2,512]{1,0:T(2,128)S(1)} %get-tuple-element.15, bf16[512,256]{0,1:T(8,128)(2,1)} %copy.47, bf16[3072,256]{0,1:T(8,128)(2,1)S(1)} %copy-done.1), kind=kOutput, calls=%fused_computation.22 | convolution fusion | flops 1890320384 | bytes 17043456 | tf_op jit(solution)/shard_map/hrk,kd->rhd/dot_general | solution.py:99
  139.3 3.5 %all-to-all-start.2 = ((bf16[4,128,512]{1,2,0:T(8,128)(2,1)}), bf16[4,128,512]{1,2,0:T(8,128)(2,1)S(1)}, u32[]{:S(2)}, u32[]{:S(2)}) async-start(bf16[4,128,512]{1,2,0:T(8,128)(2,1)} %copy.42), calls=%async_computation.2 | async-start | bytes 1048576 | tf_op jit(solution)/shard_map/all_to_all | solution.py:120
  142.8 1.9 collective-permute-start.1
  144.8 16.5 %all-gather = bf16[4,1,512]{2,1,0:T(2,128)(2,1)S(1)} all-gather(bf16[1,1,512]{2,1,0:T(2,128)(2,1)S(1)} %reshape.204), channel_id=1, replica_groups=mesh['req'=8,'tp'=4] {'tp'}, dimensions={0}, use_global_device_ids=true | all-gather | bytes 5120 | tf_op jit(solution)/shard_map/all_gather | solution.py:105
  161.4 5.3 %all-gather.1 = bf16[4,1,512]{2,1,0:T(2,128)(2,1)S(1)} all-gather(bf16[1,1,512]{2,1,0:T(2,128)(2,1)S(1)} %reshape.206), channel_id=1, replica_groups=mesh['req'=8,'tp'=4] {'tp'}, dimensions={0}, use_global_device_ids=true | all-gather | bytes 5120 | tf_op jit(solution)/shard_map/all_gather | solution.py:106
  168.8 4.7 %multiply_reduce_fusion.1 = (f32[128]{0:T(128)S(1)}, f32[128,2048]{1,0:T(8,128)S(1)}) fusion(bf16[128,2048]{0,1:T(8,128)(2,1)S(1)} %bitcast.71, bf16[2048,2048]{1,0:T(8,128)(2,1)} %all-gather.6.cloned.1.call-done), kind=kOutput, calls=%fused_computation.26 | convolution fusion | flops 1074265984 | bytes 9961984 | tf_op jit(solution)/shard_map/dot_general | solution.py:123
  173.6 1.3 add_convert_fusion.1
  174.9 2.5 %multiply_reduce_fusion = (f32[128]{0:T(128)S(1)}, f32[128,2048]{1,0:T(8,128)S(1)}) fusion(bf16[256,2048]{1,0:T(8,128)(2,1)} %all-gather.10.cloned.1.call-done, bf16[512,256]{1,0:T(8,128)(2,1)} %param.25, s32[]{:T(128)S(6)} %select_n.81, bf16[128,2048]{1,0:T(8,128)(2,1)S(1)} %add_convert_fusion.1, bf16[2048,256]{1,0:T(8,128)(2,1)} %all-gather.8.cloned.1.call-done), kind=kOutput, calls=%fused_computation.24 | convolution fusion | flops 269320064 | bytes 3736068 | tf_op jit(solution)/shard_map/dot_general | solution.py:135
  177.7 11.2 %all_to_all.49 = bf16[128,4,512]{2,0,1:T(8,128)(2,1)S(1)} all-to-all(bf16[128,4,512]{2,0,1:T(8,128)(2,1)S(1)} %bitcast.73), channel_id=1, replica_groups=mesh['req'=8,'tp'=4] {'tp'}, dimensions={1} | all-to-all | bytes 1048576 | tf_op jit(solution)/shard_map/all_to_all | solution.py:143
  (78 shorter events, 13.0 us)
Async XLA Ops:
  6.5 162.3 %all-gather.6.cloned.1.call-start = ((), (), s32[]{:S(2)}) async-start(), calls=%async_computation.4 | async-start | bytes 10485760 | tf_op jit(solution)/shard_map/all_gather | solution.py:102
  8.2 1.3 copy-start.10
  10.4 13.7 %all-to-all-start = ((s32[8,1,6]{2,1,0:T(1,128)}), s32[8,1,6]{2,1,0:T(1,128)S(1)}, u32[]{:S(2)}, u32[]{:S(2)}) async-start(s32[8,1,6]{2,1,0:T(1,128)} %copy.37), calls=%async_computation | async-start | bytes 8192 | tf_op jit(solution)/shard_map/all_to_all | solution.py:73
  26.7 6.7 %copy-start.7 = (s32[1,8]{1,0:T(1,128)S(1)}, s32[1,8]{1,0:T(1,128)}, u32[]{:S(2)}) copy-start(s32[1,8]{1,0:T(1,128)} %param.31) | copy-start | bytes 100
  26.7 6.9 %copy-start.9 = (s32[1,8]{1,0:T(1,128)S(1)}, s32[1,8]{1,0:T(1,128)}, u32[]{:S(2)}) copy-start(s32[1,8]{1,0:T(1,128)} %param.33) | copy-start | bytes 100
  26.7 73.3 %all-to-all-start.1 = ((bf16[8,6,64,512]{3,2,1,0:T(8,128)(2,1)}), bf16[8,6,64,512]{3,2,1,0:T(8,128)(2,1)S(1)}, u32[]{:S(2)}, u32[]{:S(2)}) async-start(bf16[8,6,64,512]{3,2,1,0:T(8,128)(2,1)} %bitcast.68), calls=%async_computation.1 | async-start | bytes 6291456 | tf_op jit(solution)/shard_map/all_to_all | solution.py:80
  30.5 6.4 %copy-start.8 = (s32[48,1]{0,1:T(1,128)S(1)}, s32[48,1]{0,1:T(1,128)}, u32[]{:S(2)}) copy-start(s32[48,1]{0,1:T(1,128)} %param.29) | copy-start | bytes 580
  30.5 7.7 %copy-start.6 = (s32[1,8]{1,0:T(1,128)S(1)}, s32[1,8]{1,0:T(1,128)}, u32[]{:S(2)}) copy-start(s32[1,8]{1,0:T(1,128)} %param.32) | copy-start | bytes 100
  30.5 144.4 %all-gather.10.cloned.1.call-start = ((), (), s32[]{:S(2)}) async-start(), calls=%async_computation.6 | async-start | bytes 1310720 | tf_op jit(solution)/shard_map/all_gather | solution.py:104
  33.3 133.4 %collective-permute-start = (bf16[128,512]{1,0:T(8,128)(2,1)}, bf16[128,512]{1,0:T(8,128)(2,1)S(1)}, u32[]{:S(2)}, u32[]{:S(2)}) collective-permute-start(bf16[128,512]{1,0:T(8,128)(2,1)} %get-tuple-element.10), channel_id=1, source_target_pairs={{0,1},{1,0},{2,3},{3,2},{4,5},{5,4},{6,7},{7,6},{8,9},{9,8},{10,11... | collective-permute-start | bytes 393224 | tf_op jit(solution)/shard_map/ppermute | solution.py:117
  106.3 8.6 %copy-start = (pred[512,3584]{0,1:T(8,128)(4,1)S(1)}, pred[512,3584]{0,1:T(8,128)(4,1)}, u32[]{:S(2)}) copy-start(pred[512,3584]{0,1:T(8,128)(4,1)} %pad_add_fusion) | copy-start | bytes 5505028
  114.9 16.0 %copy-start.1 = (bf16[3072,256]{0,1:T(8,128)(2,1)S(1)}, bf16[3072,256]{0,1:T(8,128)(2,1)}, u32[]{:S(2)}) copy-start(bf16[3072,256]{0,1:T(8,128)(2,1)} %copy.39) | copy-start | bytes 4718596
  138.2 4.6 %copy-start.3 = (bf16[128,512]{1,0:T(8,128)(2,1)S(1)}, bf16[128,512]{1,0:T(8,128)(2,1)}, u32[]{:S(2)}) copy-start(bf16[128,512]{1,0:T(8,128)(2,1)} %get-tuple-element.12) | copy-start | bytes 393220
  138.2 6.5 %copy-start.2 = (bf16[128,512]{1,0:T(8,128)(2,1)S(1)}, bf16[128,512]{1,0:T(8,128)(2,1)}, u32[]{:S(2)}) copy-start(bf16[128,512]{1,0:T(8,128)(2,1)} %get-tuple-element.9) | copy-start | bytes 393220
  138.2 6.5 %copy-start.4 = (bf16[512]{0:T(512)(128)(2,1)S(1)}, bf16[512]{0:T(512)(128)(2,1)}, u32[]{:S(2)}) copy-start(bf16[512]{0:T(512)(128)(2,1)} %param.24) | copy-start | bytes 3076
  138.2 23.1 %copy-start.5 = (bf16[512]{0:T(512)(128)(2,1)S(1)}, bf16[512]{0:T(512)(128)(2,1)}, u32[]{:S(2)}) copy-start(bf16[512]{0:T(512)(128)(2,1)} %param.28) | copy-start | bytes 3076
  139.3 29.6 %all-to-all-start.2 = ((bf16[4,128,512]{1,2,0:T(8,128)(2,1)}), bf16[4,128,512]{1,2,0:T(8,128)(2,1)S(1)}, u32[]{:S(2)}, u32[]{:S(2)}) async-start(bf16[4,128,512]{1,2,0:T(8,128)(2,1)} %copy.42), calls=%async_computation.2 | async-start | bytes 1048576 | tf_op jit(solution)/shard_map/all_to_all | solution.py:120
  142.7 32.2 %all-gather.8.cloned.1.call-start = ((), (), s32[]{:S(2)}) async-start(), calls=%async_computation.5 | async-start | bytes 1310720 | tf_op jit(solution)/shard_map/all_gather | solution.py:103
  142.8 24.7 %collective-permute-start.1 = (bf16[128,512]{1,0:T(8,128)(2,1)S(1)}, bf16[128,512]{1,0:T(8,128)(2,1)S(1)}, u32[]{:S(2)}, u32[]{:S(2)}) collective-permute-start(bf16[128,512]{1,0:T(8,128)(2,1)S(1)} %copy-done.3), channel_id=1, source_target_pairs={{0,2},{1,3},{2,0},{3,1},{4,6},{5,7},{6,4},{7,5},{8,10},{9,11},{10,... | collective-permute-start | bytes 393224 | tf_op jit(solution)/shard_map/ppermute | solution.py:117
  144.7 23.4 %collective-permute-start.2 = (bf16[128,512]{1,0:T(8,128)(2,1)S(1)}, bf16[128,512]{1,0:T(8,128)(2,1)S(1)}, u32[]{:S(2)}, u32[]{:S(2)}) collective-permute-start(bf16[128,512]{1,0:T(8,128)(2,1)S(1)} %copy-done.2), channel_id=1, source_target_pairs={{0,3},{1,2},{2,1},{3,0},{4,7},{5,6},{6,5},{7,4},{8,11},{9,10},{10,... | collective-permute-start | bytes 393224 | tf_op jit(solution)/shard_map/ppermute | solution.py:117
Sparse Core Ops, SparseCore 0:
  8.9 60.9 all-gather.5
  71.5 16.7 all-gather.9
  145.1 19.1 all-gather.7
